TPU v7x, 512 devices: a whole 4x4x16 slice. The times are simulated.
512 devices in a mesh: ctx: 32 (over x, y, core), head: 16 (over z).
Axes of the slice: x: 4, y: 4, z: 16, core: 2. Of those that a mesh axis runs over, the one named last changes fastest.
Arguments:
- q_linear: bfloat16 [8192, 8192], P('ctx', 'head'), may hold values from -4 to 4
- k_linear: bfloat16 [8192, 8192], P('ctx', 'head'), may hold values from -4 to 4
- v_linear: bfloat16 [8192, 8192], P('ctx', 'head'), may hold values from -40 to 40
- log_decay: float32 [8192, 64], P('ctx', 'head'), may hold values from -1 to 0
- norm_gain: float32 [8192], P('head'), may hold values from 0.5 to 1.5
- q_soft: bfloat16 [8192, 8192], P('ctx', 'head'), may hold values from -6 to 6
- k_soft: bfloat16 [8192, 1024], P('ctx'), may hold values from -4 to 4
- v_soft: bfloat16 [8192, 1024], P('ctx'), may hold values from -4 to 4
Outputs:
- linear_out: bfloat16 [8192, 8192], P('ctx', 'head')
- soft_out: bfloat16 [8192, 8192], P('ctx', 'head')
All inputs are finite; a program needn't handle non-finite values.
Results may differ from a plain program's by a relative error of at most 0.0075.
Values may be sent and summed in bfloat16 or wider, within the bound.
No kernel may reach another device: no remote copies, remote signals or barrier semaphores. Data moves between devices by JAX's collectives and lax.ppermute only.
A program may use at most 64 MiB of HBM per device.

v0:
```python
import jax
import jax.numpy as jnp
from jax import lax
from jax.sharding import PartitionSpec as P

QUERY_HEADS = 64
DH = 128
KV_HEADS = 8
BLOCK = 256
EPSILON = 1e-06
NEGATIVE = -1e30


def shifted(value, axis, steps):
    count = lax.axis_size(axis)
    first, last = (max(0, -steps), min(count, count - steps))
    return lax.ppermute(value, axis, [(source, source + steps) for source in range(first, last)])


def lightning_step(carry, inputs):
    running, log_before = carry
    queries, key_rows, value_rows, log_gates = inputs
    row_count = queries.shape[0]
    cumulative = jnp.cumsum(log_gates, axis=0)
    final_log = cumulative[-1]
    positions = jnp.arange(row_count, dtype=jnp.int32)
    causal = positions[None, :] <= positions[:, None]
    cum_heads = cumulative.T
    log_gap = jnp.where(causal[None], cum_heads[:, :, None] - cum_heads[:, None, :], NEGATIVE)
    scores = jnp.einsum("thd,shd->hts", queries, key_rows, preferred_element_type=jnp.float32)
    weights = (scores * jnp.exp(log_gap)).astype(jnp.bfloat16)
    intra_part = jnp.einsum("hts,she->the", weights, value_rows, preferred_element_type=jnp.float32)
    query_wide = queries.astype(jnp.float32)
    lifted_here = query_wide * jnp.exp(cumulative)[:, :, None]
    carried_here = jnp.einsum("thd,hde->the", lifted_here, running, precision=lax.Precision.HIGHEST)
    lifted_device = query_wide * jnp.exp(cumulative + log_before[None, :])[:, :, None]
    scaled = (key_rows * jnp.exp(final_log[None, :] - cumulative)[:, :, None]).astype(jnp.bfloat16)
    block_state = jnp.einsum("shd,she->hde", scaled, value_rows, preferred_element_type=jnp.float32)
    running = jnp.exp(final_log)[:, None, None] * running + block_state
    return ((running, log_before + final_log), (intra_part + carried_here, lifted_device))


def soft_update(running, queries, query_pos, key_rows, value_rows, key_pos):
    row_max, row_total, weighted = running
    head_count, row_count = row_max.shape
    kv_count, group_local = (queries.shape[1], queries.shape[2])
    scores = jnp.einsum("tkgd,skd->kgts", queries, key_rows, preferred_element_type=jnp.float32)
    scores = scores.reshape(head_count, row_count, key_rows.shape[0]) * DH ** (-0.5)
    allowed = key_pos[None, :] <= query_pos[:, None]
    scores = jnp.where(allowed[None], scores, NEGATIVE)
    new_max = jnp.maximum(row_max, jnp.max(scores, axis=2))
    probabilities = jnp.where(allowed[None], jnp.exp(scores - new_max[:, :, None]), 0.0)
    rescale = jnp.exp(row_max - new_max)
    row_total = row_total * rescale + jnp.sum(probabilities, axis=2)
    rounded = probabilities.astype(jnp.bfloat16).reshape(
        kv_count, group_local, row_count, key_rows.shape[0]
    )
    product = jnp.einsum(
        "kgts,ske->kgte", rounded, value_rows, preferred_element_type=jnp.float32
    ).reshape(head_count, row_count, DH)
    weighted = weighted * rescale[:, :, None] + product
    return (new_max, row_total, weighted)


def over_blocks(running, pieces, row_count, visitor):
    key_rows, value_rows = pieces

    def one_block(block_index, inner_state):
        block_start = block_index * row_count
        keys_here = lax.dynamic_slice_in_dim(key_rows, block_start, row_count, 0)
        values_here = lax.dynamic_slice_in_dim(value_rows, block_start, row_count, 0)
        return visitor(inner_state, keys_here, values_here, block_start)

    return lax.fori_loop(0, key_rows.shape[0] // row_count, one_block, running)


def finish(row_total, weighted, row_count, width):
    return (
        jnp.transpose(weighted / row_total[:, :, None], (1, 0, 2))
        .reshape(row_count, width)
        .astype(jnp.bfloat16)
    )


def local(q_linear, k_linear, v_linear, log_decay, norm_gain, q_soft, k_soft, v_soft):
    row_count = q_linear.shape[0]
    head_count = log_decay.shape[1]
    width = head_count * DH
    local_blocks = row_count // BLOCK
    lin_shape = (local_blocks, BLOCK, head_count, DH)
    sequences = (
        q_linear.reshape(lin_shape),
        k_linear.reshape(lin_shape),
        v_linear.reshape(lin_shape),
        log_decay.reshape(local_blocks, BLOCK, head_count),
    )
    start_carry = (
        jnp.zeros((head_count, DH, DH), jnp.float32),
        jnp.zeros((head_count,), jnp.float32),
    )
    (block_state, log_total), (local_part, lifted) = lax.scan(
        lightning_step, start_carry, sequences
    )
    local_part = local_part.reshape(row_count, head_count, DH)
    lifted = lifted.reshape(row_count, head_count, DH)
    block_fade = jnp.exp(log_total)

    def advance(step_index, entering):
        leaving = block_fade[:, None, None] * entering + block_state
        return shifted(leaving, "ctx", 1)

    entering = lax.fori_loop(0, lax.axis_size("ctx") - 1, advance, jnp.zeros_like(block_state))
    carried = jnp.einsum("thd,hde->the", lifted, entering, precision=lax.Precision.HIGHEST)
    mixed = (local_part + carried).reshape(row_count, width)
    power = lax.psum(jnp.sum(mixed * mixed, axis=1), "head") / (QUERY_HEADS * DH)
    linear_out = (mixed * lax.rsqrt(power + EPSILON)[:, None] * norm_gain[None, :]).astype(
        jnp.bfloat16
    )
    group_size = QUERY_HEADS // KV_HEADS
    kv_count = max(1, head_count // group_size)
    group_local = head_count // kv_count
    kv_start = lax.axis_index("head") * head_count // group_size
    k_local = lax.dynamic_slice_in_dim(k_soft, kv_start * DH, kv_count * DH, 1)
    v_local = lax.dynamic_slice_in_dim(v_soft, kv_start * DH, kv_count * DH, 1)
    query_shape = (row_count, kv_count, group_local, DH)
    key_shape = (row_count, kv_count, DH)
    my_index = lax.axis_index("ctx")
    positions = jnp.arange(row_count, dtype=jnp.int32)
    initial = (
        jnp.full((head_count, row_count), NEGATIVE, jnp.float32),
        jnp.zeros((head_count, row_count), jnp.float32),
        jnp.zeros((head_count, row_count, DH), jnp.float32),
    )
    queries = q_soft.reshape(query_shape)
    query_pos = my_index * row_count + positions
    query_end = my_index * row_count + row_count - 1

    def visitor(running, keys_here, values_here, block_start):
        return lax.cond(
            block_start <= query_end,
            lambda state: soft_update(
                state,
                queries,
                query_pos,
                keys_here.reshape(key_shape),
                values_here.reshape(key_shape),
                block_start + positions,
            ),
            lambda state: state,
            running,
        )

    row_max, row_total, weighted = over_blocks(
        initial,
        (
            lax.all_gather(k_local, "ctx", axis=0, tiled=True),
            lax.all_gather(v_local, "ctx", axis=0, tiled=True),
        ),
        row_count,
        visitor,
    )
    soft_out = finish(row_total, weighted, row_count, width)
    return (linear_out, soft_out)


def solution(mesh):
    return jax.shard_map(
        local,
        mesh=mesh,
        in_specs=(
            P("ctx", "head"),
            P("ctx", "head"),
            P("ctx", "head"),
            P("ctx", "head"),
            P("head"),
            P("ctx", "head"),
            P("ctx", None),
            P("ctx", None),
        ),
        out_specs=(P("ctx", "head"), P("ctx", "head")),
        check_vma=False,
    )
```

profile of v0, /device:TPU:6, one launch (start us, length us, event | category | flops | bytes accessed | tf_op | source)
XLA Modules:
  0.0 451.1 jit_solution(13501809953526398341)
XLA Ops:
  16.4 310.2 %while.9 = (s32[]{:T(128)}, f32[4,128,128]{2,1,0:T(8,128)S(1)}, f32[4]{0:T(128)S(1)}, f32[4,128,128]{2,1,0:T(8,128)S(1)}, s32[]{:T(128)}) while((s32[]{:T(128)}, f32[4,128,128]{2,1,0:T(8,128)S(1)}, f32[4]{0:T(128)S(1)}, f32[4,128,128]{2,1,0:T(8,128)S(1)}, s32[]{:T(128)}) %tuple.85), condition=%wide.region_3.4_spmd, body=%wide.region_2.3_spmd.sunk | while | flops 131074 | bytes 1835125 | solution.py:112
  18.5 7.9 %collective-permute-done = f32[4,128,128]{2,1,0:T(8,128)S(1)} collective-permute-done((f32[4,128,128]{2,1,0:T(8,128)S(1)}, f32[4,128,128]{2,1,0:T(8,128)S(1)}, u32[]{:S(2)}, u32[]{:S(2)}) %collective-permute-start) | collective-permute-done | bytes 262176 | tf_op jit(solution)/shard_map/while/body/eval_jaxpr/ppermute | solution.py:17
  26.4 1.9 collective-permute-start
  28.4 7.9 %collective-permute-done = f32[4,128,128]{2,1,0:T(8,128)S(1)} collective-permute-done((f32[4,128,128]{2,1,0:T(8,128)S(1)}, f32[4,128,128]{2,1,0:T(8,128)S(1)}, u32[]{:S(2)}, u32[]{:S(2)}) %collective-permute-start) | collective-permute-done | bytes 262176 | tf_op jit(solution)/shard_map/while/body/eval_jaxpr/ppermute | solution.py:17
  38.3 8.0 %collective-permute-done = f32[4,128,128]{2,1,0:T(8,128)S(1)} collective-permute-done((f32[4,128,128]{2,1,0:T(8,128)S(1)}, f32[4,128,128]{2,1,0:T(8,128)S(1)}, u32[]{:S(2)}, u32[]{:S(2)}) %collective-permute-start) | collective-permute-done | bytes 262176 | tf_op jit(solution)/shard_map/while/body/eval_jaxpr/ppermute | solution.py:17
  46.4 1.9 collective-permute-start
  48.3 7.9 %collective-permute-done = f32[4,128,128]{2,1,0:T(8,128)S(1)} collective-permute-done((f32[4,128,128]{2,1,0:T(8,128)S(1)}, f32[4,128,128]{2,1,0:T(8,128)S(1)}, u32[]{:S(2)}, u32[]{:S(2)}) %collective-permute-start) | collective-permute-done | bytes 262176 | tf_op jit(solution)/shard_map/while/body/eval_jaxpr/ppermute | solution.py:17
  56.3 1.9 collective-permute-start
  58.2 8.4 %collective-permute-done = f32[4,128,128]{2,1,0:T(8,128)S(1)} collective-permute-done((f32[4,128,128]{2,1,0:T(8,128)S(1)}, f32[4,128,128]{2,1,0:T(8,128)S(1)}, u32[]{:S(2)}, u32[]{:S(2)}) %collective-permute-start) | collective-permute-done | bytes 262176 | tf_op jit(solution)/shard_map/while/body/eval_jaxpr/ppermute | solution.py:17
  68.6 8.7 %collective-permute-done = f32[4,128,128]{2,1,0:T(8,128)S(1)} collective-permute-done((f32[4,128,128]{2,1,0:T(8,128)S(1)}, f32[4,128,128]{2,1,0:T(8,128)S(1)}, u32[]{:S(2)}, u32[]{:S(2)}) %collective-permute-start) | collective-permute-done | bytes 262176 | tf_op jit(solution)/shard_map/while/body/eval_jaxpr/ppermute | solution.py:17
  79.4 7.9 %collective-permute-done = f32[4,128,128]{2,1,0:T(8,128)S(1)} collective-permute-done((f32[4,128,128]{2,1,0:T(8,128)S(1)}, f32[4,128,128]{2,1,0:T(8,128)S(1)}, u32[]{:S(2)}, u32[]{:S(2)}) %collective-permute-start) | collective-permute-done | bytes 262176 | tf_op jit(solution)/shard_map/while/body/eval_jaxpr/ppermute | solution.py:17
  87.4 1.9 collective-permute-start
  89.3 7.9 %collective-permute-done = f32[4,128,128]{2,1,0:T(8,128)S(1)} collective-permute-done((f32[4,128,128]{2,1,0:T(8,128)S(1)}, f32[4,128,128]{2,1,0:T(8,128)S(1)}, u32[]{:S(2)}, u32[]{:S(2)}) %collective-permute-start) | collective-permute-done | bytes 262176 | tf_op jit(solution)/shard_map/while/body/eval_jaxpr/ppermute | solution.py:17
  99.2 8.3 %collective-permute-done = f32[4,128,128]{2,1,0:T(8,128)S(1)} collective-permute-done((f32[4,128,128]{2,1,0:T(8,128)S(1)}, f32[4,128,128]{2,1,0:T(8,128)S(1)}, u32[]{:S(2)}, u32[]{:S(2)}) %collective-permute-start) | collective-permute-done | bytes 262176 | tf_op jit(solution)/shard_map/while/body/eval_jaxpr/ppermute | solution.py:17
  107.6 1.9 collective-permute-start
  109.5 7.9 %collective-permute-done = f32[4,128,128]{2,1,0:T(8,128)S(1)} collective-permute-done((f32[4,128,128]{2,1,0:T(8,128)S(1)}, f32[4,128,128]{2,1,0:T(8,128)S(1)}, u32[]{:S(2)}, u32[]{:S(2)}) %collective-permute-start) | collective-permute-done | bytes 262176 | tf_op jit(solution)/shard_map/while/body/eval_jaxpr/ppermute | solution.py:17
  119.4 7.9 %collective-permute-done = f32[4,128,128]{2,1,0:T(8,128)S(1)} collective-permute-done((f32[4,128,128]{2,1,0:T(8,128)S(1)}, f32[4,128,128]{2,1,0:T(8,128)S(1)}, u32[]{:S(2)}, u32[]{:S(2)}) %collective-permute-start) | collective-permute-done | bytes 262176 | tf_op jit(solution)/shard_map/while/body/eval_jaxpr/ppermute | solution.py:17
  129.3 9.3 %collective-permute-done = f32[4,128,128]{2,1,0:T(8,128)S(1)} collective-permute-done((f32[4,128,128]{2,1,0:T(8,128)S(1)}, f32[4,128,128]{2,1,0:T(8,128)S(1)}, u32[]{:S(2)}, u32[]{:S(2)}) %collective-permute-start) | collective-permute-done | bytes 262176 | tf_op jit(solution)/shard_map/while/body/eval_jaxpr/ppermute | solution.py:17
  140.6 7.9 %collective-permute-done = f32[4,128,128]{2,1,0:T(8,128)S(1)} collective-permute-done((f32[4,128,128]{2,1,0:T(8,128)S(1)}, f32[4,128,128]{2,1,0:T(8,128)S(1)}, u32[]{:S(2)}, u32[]{:S(2)}) %collective-permute-start) | collective-permute-done | bytes 262176 | tf_op jit(solution)/shard_map/while/body/eval_jaxpr/ppermute | solution.py:17
  150.5 7.9 %collective-permute-done = f32[4,128,128]{2,1,0:T(8,128)S(1)} collective-permute-done((f32[4,128,128]{2,1,0:T(8,128)S(1)}, f32[4,128,128]{2,1,0:T(8,128)S(1)}, u32[]{:S(2)}, u32[]{:S(2)}) %collective-permute-start) | collective-permute-done | bytes 262176 | tf_op jit(solution)/shard_map/while/body/eval_jaxpr/ppermute | solution.py:17
  160.4 7.9 %collective-permute-done = f32[4,128,128]{2,1,0:T(8,128)S(1)} collective-permute-done((f32[4,128,128]{2,1,0:T(8,128)S(1)}, f32[4,128,128]{2,1,0:T(8,128)S(1)}, u32[]{:S(2)}, u32[]{:S(2)}) %collective-permute-start) | collective-permute-done | bytes 262176 | tf_op jit(solution)/shard_map/while/body/eval_jaxpr/ppermute | solution.py:17
  170.3 7.9 %collective-permute-done = f32[4,128,128]{2,1,0:T(8,128)S(1)} collective-permute-done((f32[4,128,128]{2,1,0:T(8,128)S(1)}, f32[4,128,128]{2,1,0:T(8,128)S(1)}, u32[]{:S(2)}, u32[]{:S(2)}) %collective-permute-start) | collective-permute-done | bytes 262176 | tf_op jit(solution)/shard_map/while/body/eval_jaxpr/ppermute | solution.py:17
  180.2 7.9 %collective-permute-done = f32[4,128,128]{2,1,0:T(8,128)S(1)} collective-permute-done((f32[4,128,128]{2,1,0:T(8,128)S(1)}, f32[4,128,128]{2,1,0:T(8,128)S(1)}, u32[]{:S(2)}, u32[]{:S(2)}) %collective-permute-start) | collective-permute-done | bytes 262176 | tf_op jit(solution)/shard_map/while/body/eval_jaxpr/ppermute | solution.py:17
  190.1 7.9 %collective-permute-done = f32[4,128,128]{2,1,0:T(8,128)S(1)} collective-permute-done((f32[4,128,128]{2,1,0:T(8,128)S(1)}, f32[4,128,128]{2,1,0:T(8,128)S(1)}, u32[]{:S(2)}, u32[]{:S(2)}) %collective-permute-start) | collective-permute-done | bytes 262176 | tf_op jit(solution)/shard_map/while/body/eval_jaxpr/ppermute | solution.py:17
  200.0 7.9 %collective-permute-done = f32[4,128,128]{2,1,0:T(8,128)S(1)} collective-permute-done((f32[4,128,128]{2,1,0:T(8,128)S(1)}, f32[4,128,128]{2,1,0:T(8,128)S(1)}, u32[]{:S(2)}, u32[]{:S(2)}) %collective-permute-start) | collective-permute-done | bytes 262176 | tf_op jit(solution)/shard_map/while/body/eval_jaxpr/ppermute | solution.py:17
  209.9 7.9 %collective-permute-done = f32[4,128,128]{2,1,0:T(8,128)S(1)} collective-permute-done((f32[4,128,128]{2,1,0:T(8,128)S(1)}, f32[4,128,128]{2,1,0:T(8,128)S(1)}, u32[]{:S(2)}, u32[]{:S(2)}) %collective-permute-start) | collective-permute-done | bytes 262176 | tf_op jit(solution)/shard_map/while/body/eval_jaxpr/ppermute | solution.py:17
  219.8 7.9 %collective-permute-done = f32[4,128,128]{2,1,0:T(8,128)S(1)} collective-permute-done((f32[4,128,128]{2,1,0:T(8,128)S(1)}, f32[4,128,128]{2,1,0:T(8,128)S(1)}, u32[]{:S(2)}, u32[]{:S(2)}) %collective-permute-start) | collective-permute-done | bytes 262176 | tf_op jit(solution)/shard_map/while/body/eval_jaxpr/ppermute | solution.py:17
  229.7 7.9 %collective-permute-done = f32[4,128,128]{2,1,0:T(8,128)S(1)} collective-permute-done((f32[4,128,128]{2,1,0:T(8,128)S(1)}, f32[4,128,128]{2,1,0:T(8,128)S(1)}, u32[]{:S(2)}, u32[]{:S(2)}) %collective-permute-start) | collective-permute-done | bytes 262176 | tf_op jit(solution)/shard_map/while/body/eval_jaxpr/ppermute | solution.py:17
  239.6 7.9 %collective-permute-done = f32[4,128,128]{2,1,0:T(8,128)S(1)} collective-permute-done((f32[4,128,128]{2,1,0:T(8,128)S(1)}, f32[4,128,128]{2,1,0:T(8,128)S(1)}, u32[]{:S(2)}, u32[]{:S(2)}) %collective-permute-start) | collective-permute-done | bytes 262176 | tf_op jit(solution)/shard_map/while/body/eval_jaxpr/ppermute | solution.py:17
  249.5 7.9 %collective-permute-done = f32[4,128,128]{2,1,0:T(8,128)S(1)} collective-permute-done((f32[4,128,128]{2,1,0:T(8,128)S(1)}, f32[4,128,128]{2,1,0:T(8,128)S(1)}, u32[]{:S(2)}, u32[]{:S(2)}) %collective-permute-start) | collective-permute-done | bytes 262176 | tf_op jit(solution)/shard_map/while/body/eval_jaxpr/ppermute | solution.py:17
  259.4 7.9 %collective-permute-done = f32[4,128,128]{2,1,0:T(8,128)S(1)} collective-permute-done((f32[4,128,128]{2,1,0:T(8,128)S(1)}, f32[4,128,128]{2,1,0:T(8,128)S(1)}, u32[]{:S(2)}, u32[]{:S(2)}) %collective-permute-start) | collective-permute-done | bytes 262176 | tf_op jit(solution)/shard_map/while/body/eval_jaxpr/ppermute | solution.py:17
  269.3 7.9 %collective-permute-done = f32[4,128,128]{2,1,0:T(8,128)S(1)} collective-permute-done((f32[4,128,128]{2,1,0:T(8,128)S(1)}, f32[4,128,128]{2,1,0:T(8,128)S(1)}, u32[]{:S(2)}, u32[]{:S(2)}) %collective-permute-start) | collective-permute-done | bytes 262176 | tf_op jit(solution)/shard_map/while/body/eval_jaxpr/ppermute | solution.py:17
  279.2 7.9 %collective-permute-done = f32[4,128,128]{2,1,0:T(8,128)S(1)} collective-permute-done((f32[4,128,128]{2,1,0:T(8,128)S(1)}, f32[4,128,128]{2,1,0:T(8,128)S(1)}, u32[]{:S(2)}, u32[]{:S(2)}) %collective-permute-start) | collective-permute-done | bytes 262176 | tf_op jit(solution)/shard_map/while/body/eval_jaxpr/ppermute | solution.py:17
  289.1 7.9 %collective-permute-done = f32[4,128,128]{2,1,0:T(8,128)S(1)} collective-permute-done((f32[4,128,128]{2,1,0:T(8,128)S(1)}, f32[4,128,128]{2,1,0:T(8,128)S(1)}, u32[]{:S(2)}, u32[]{:S(2)}) %collective-permute-start) | collective-permute-done | bytes 262176 | tf_op jit(solution)/shard_map/while/body/eval_jaxpr/ppermute | solution.py:17
  299.0 7.9 %collective-permute-done = f32[4,128,128]{2,1,0:T(8,128)S(1)} collective-permute-done((f32[4,128,128]{2,1,0:T(8,128)S(1)}, f32[4,128,128]{2,1,0:T(8,128)S(1)}, u32[]{:S(2)}, u32[]{:S(2)}) %collective-permute-start) | collective-permute-done | bytes 262176 | tf_op jit(solution)/shard_map/while/body/eval_jaxpr/ppermute | solution.py:17
  308.9 7.9 %collective-permute-done = f32[4,128,128]{2,1,0:T(8,128)S(1)} collective-permute-done((f32[4,128,128]{2,1,0:T(8,128)S(1)}, f32[4,128,128]{2,1,0:T(8,128)S(1)}, u32[]{:S(2)}, u32[]{:S(2)}) %collective-permute-start) | collective-permute-done | bytes 262176 | tf_op jit(solution)/shard_map/while/body/eval_jaxpr/ppermute | solution.py:17
  318.8 7.9 %collective-permute-done = f32[4,128,128]{2,1,0:T(8,128)S(1)} collective-permute-done((f32[4,128,128]{2,1,0:T(8,128)S(1)}, f32[4,128,128]{2,1,0:T(8,128)S(1)}, u32[]{:S(2)}, u32[]{:S(2)}) %collective-permute-start) | collective-permute-done | bytes 262176 | tf_op jit(solution)/shard_map/while/body/eval_jaxpr/ppermute | solution.py:17
  328.2 37.5 %psum.7 = f32[256]{0:T(256)S(1)} all-reduce(f32[256]{0:T(256)S(1)} %get-tuple-element.439), channel_id=1, replica_groups=mesh['ctx'=32,'head'=16] {'head'}, use_global_device_ids=true, to_apply=%region_5.6 | all-reduce | flops 256 | bytes 2048 | tf_op jit(solution)/shard_map/psum | solution.py:115
  366.6 76.8 %while.36 = (s32[]{:T(128)}, f32[4,256]{1,0:T(4,128)S(1)}, f32[4,256]{1,0:T(4,128)S(1)}, f32[4,256,128]{2,1,0:T(8,128)S(1)}, s32[]{:T(128)}, /*index=5*/bf16[819...) while((s32[]{:T(128)}, f32[4,256]{1,0:T(4,128)S(1)}, ...), condition=%wide.region_11.12_spmd.clone, body=%wide.region_6.11_spmd.clone.sunk | while | flops 137431552 | bytes 4922689 | solution.py:74
  366.6 3.0 conditional.3
  369.7 3.0 conditional.3
  372.7 3.0 conditional.3
  375.8 3.0 conditional.3
  378.8 3.0 conditional.3
  381.9 3.0 conditional.3
  384.9 3.0 conditional.3
  388.0 3.0 conditional.3
  391.1 3.0 conditional.3
  394.1 3.0 conditional.3
  397.2 3.0 conditional.3
  400.2 3.0 conditional.3
  403.3 3.0 conditional.3
  406.3 3.0 conditional.3
  409.4 3.0 conditional.3
  412.5 3.0 conditional.3
  415.5 3.0 conditional.3
  418.6 3.0 conditional.3
  421.6 3.0 conditional.3
  424.7 3.0 conditional.3
  427.7 3.0 conditional.3
  430.8 3.0 conditional.3
  433.9 3.0 conditional.3
  436.9 3.0 conditional.3
  440.0 3.0 conditional.3
  (340 shorter events, 139.1 us)
Async XLA Ops:
  7.2 1.0 copy-start
  7.2 8.2 %copy-start.1 = (bf16[256,512]{1,0:T(8,128)(2,1)S(1)}, bf16[256,512]{1,0:T(8,128)(2,1)}, u32[]{:S(2)}) copy-start(bf16[256,512]{1,0:T(8,128)(2,1)} %param.14) | copy-start | bytes 786436
  7.2 9.0 %copy-start.2 = (bf16[256,512]{1,0:T(8,128)(2,1)S(1)}, bf16[256,512]{1,0:T(8,128)(2,1)}, u32[]{:S(2)}) copy-start(bf16[256,512]{1,0:T(8,128)(2,1)} %param.16) | copy-start | bytes 786436
  7.2 359.3 %all-gather.3.cloned.1.call-start = ((), (), s32[]{:S(2)}) async-start(), calls=%async_computation | async-start | bytes 2162688 | tf_op jit(solution)/shard_map/all_gather | solution.py:156
  8.9 357.6 %all-gather.5.cloned.1.call-start = ((), (), s32[]{:S(2)}) async-start(), calls=%async_computation.1 | async-start | bytes 2162688 | tf_op jit(solution)/shard_map/all_gather | solution.py:157
  16.5 9.8 %collective-permute-start = (f32[4,128,128]{2,1,0:T(8,128)S(1)}, f32[4,128,128]{2,1,0:T(8,128)S(1)}, u32[]{:S(2)}, u32[]{:S(2)}) collective-permute-start(f32[4,128,128]{2,1,0:T(8,128)S(1)} %multiply_add_fusion.3), channel_id=1, source_target_pairs={{0,16},{16,32},{32,48},{48,64},{64,80},{80,96},{96,112},{112,128},... | collective-permute-start | bytes 786440 | tf_op jit(solution)/shard_map/while/body/eval_jaxpr/ppermute | solution.py:17
  26.4 9.8 %collective-permute-start = (f32[4,128,128]{2,1,0:T(8,128)S(1)}, f32[4,128,128]{2,1,0:T(8,128)S(1)}, u32[]{:S(2)}, u32[]{:S(2)}) collective-permute-start(f32[4,128,128]{2,1,0:T(8,128)S(1)} %multiply_add_fusion.3), channel_id=1, source_target_pairs={{0,16},{16,32},{32,48},{48,64},{64,80},{80,96},{96,112},{112,128},... | collective-permute-start | bytes 786440 | tf_op jit(solution)/shard_map/while/body/eval_jaxpr/ppermute | solution.py:17
  36.3 10.0 %collective-permute-start = (f32[4,128,128]{2,1,0:T(8,128)S(1)}, f32[4,128,128]{2,1,0:T(8,128)S(1)}, u32[]{:S(2)}, u32[]{:S(2)}) collective-permute-start(f32[4,128,128]{2,1,0:T(8,128)S(1)} %multiply_add_fusion.3), channel_id=1, source_target_pairs={{0,16},{16,32},{32,48},{48,64},{64,80},{80,96},{96,112},{112,128},... | collective-permute-start | bytes 786440 | tf_op jit(solution)/shard_map/while/body/eval_jaxpr/ppermute | solution.py:17
  46.4 9.8 %collective-permute-start = (f32[4,128,128]{2,1,0:T(8,128)S(1)}, f32[4,128,128]{2,1,0:T(8,128)S(1)}, u32[]{:S(2)}, u32[]{:S(2)}) collective-permute-start(f32[4,128,128]{2,1,0:T(8,128)S(1)} %multiply_add_fusion.3), channel_id=1, source_target_pairs={{0,16},{16,32},{32,48},{48,64},{64,80},{80,96},{96,112},{112,128},... | collective-permute-start | bytes 786440 | tf_op jit(solution)/shard_map/while/body/eval_jaxpr/ppermute | solution.py:17
  56.3 10.3 %collective-permute-start = (f32[4,128,128]{2,1,0:T(8,128)S(1)}, f32[4,128,128]{2,1,0:T(8,128)S(1)}, u32[]{:S(2)}, u32[]{:S(2)}) collective-permute-start(f32[4,128,128]{2,1,0:T(8,128)S(1)} %multiply_add_fusion.3), channel_id=1, source_target_pairs={{0,16},{16,32},{32,48},{48,64},{64,80},{80,96},{96,112},{112,128},... | collective-permute-start | bytes 786440 | tf_op jit(solution)/shard_map/while/body/eval_jaxpr/ppermute | solution.py:17
  66.7 10.7 %collective-permute-start = (f32[4,128,128]{2,1,0:T(8,128)S(1)}, f32[4,128,128]{2,1,0:T(8,128)S(1)}, u32[]{:S(2)}, u32[]{:S(2)}) collective-permute-start(f32[4,128,128]{2,1,0:T(8,128)S(1)} %multiply_add_fusion.3), channel_id=1, source_target_pairs={{0,16},{16,32},{32,48},{48,64},{64,80},{80,96},{96,112},{112,128},... | collective-permute-start | bytes 786440 | tf_op jit(solution)/shard_map/while/body/eval_jaxpr/ppermute | solution.py:17
  77.5 9.8 %collective-permute-start = (f32[4,128,128]{2,1,0:T(8,128)S(1)}, f32[4,128,128]{2,1,0:T(8,128)S(1)}, u32[]{:S(2)}, u32[]{:S(2)}) collective-permute-start(f32[4,128,128]{2,1,0:T(8,128)S(1)} %multiply_add_fusion.3), channel_id=1, source_target_pairs={{0,16},{16,32},{32,48},{48,64},{64,80},{80,96},{96,112},{112,128},... | collective-permute-start | bytes 786440 | tf_op jit(solution)/shard_map/while/body/eval_jaxpr/ppermute | solution.py:17
  87.4 9.8 %collective-permute-start = (f32[4,128,128]{2,1,0:T(8,128)S(1)}, f32[4,128,128]{2,1,0:T(8,128)S(1)}, u32[]{:S(2)}, u32[]{:S(2)}) collective-permute-start(f32[4,128,128]{2,1,0:T(8,128)S(1)} %multiply_add_fusion.3), channel_id=1, source_target_pairs={{0,16},{16,32},{32,48},{48,64},{64,80},{80,96},{96,112},{112,128},... | collective-permute-start | bytes 786440 | tf_op jit(solution)/shard_map/while/body/eval_jaxpr/ppermute | solution.py:17
  97.3 10.2 %collective-permute-start = (f32[4,128,128]{2,1,0:T(8,128)S(1)}, f32[4,128,128]{2,1,0:T(8,128)S(1)}, u32[]{:S(2)}, u32[]{:S(2)}) collective-permute-start(f32[4,128,128]{2,1,0:T(8,128)S(1)} %multiply_add_fusion.3), channel_id=1, source_target_pairs={{0,16},{16,32},{32,48},{48,64},{64,80},{80,96},{96,112},{112,128},... | collective-permute-start | bytes 786440 | tf_op jit(solution)/shard_map/while/body/eval_jaxpr/ppermute | solution.py:17
  107.6 9.8 %collective-permute-start = (f32[4,128,128]{2,1,0:T(8,128)S(1)}, f32[4,128,128]{2,1,0:T(8,128)S(1)}, u32[]{:S(2)}, u32[]{:S(2)}) collective-permute-start(f32[4,128,128]{2,1,0:T(8,128)S(1)} %multiply_add_fusion.3), channel_id=1, source_target_pairs={{0,16},{16,32},{32,48},{48,64},{64,80},{80,96},{96,112},{112,128},... | collective-permute-start | bytes 786440 | tf_op jit(solution)/shard_map/while/body/eval_jaxpr/ppermute | solution.py:17
  117.5 9.8 %collective-permute-start = (f32[4,128,128]{2,1,0:T(8,128)S(1)}, f32[4,128,128]{2,1,0:T(8,128)S(1)}, u32[]{:S(2)}, u32[]{:S(2)}) collective-permute-start(f32[4,128,128]{2,1,0:T(8,128)S(1)} %multiply_add_fusion.3), channel_id=1, source_target_pairs={{0,16},{16,32},{32,48},{48,64},{64,80},{80,96},{96,112},{112,128},... | collective-permute-start | bytes 786440 | tf_op jit(solution)/shard_map/while/body/eval_jaxpr/ppermute | solution.py:17
  127.4 11.2 %collective-permute-start = (f32[4,128,128]{2,1,0:T(8,128)S(1)}, f32[4,128,128]{2,1,0:T(8,128)S(1)}, u32[]{:S(2)}, u32[]{:S(2)}) collective-permute-start(f32[4,128,128]{2,1,0:T(8,128)S(1)} %multiply_add_fusion.3), channel_id=1, source_target_pairs={{0,16},{16,32},{32,48},{48,64},{64,80},{80,96},{96,112},{112,128},... | collective-permute-start | bytes 786440 | tf_op jit(solution)/shard_map/while/body/eval_jaxpr/ppermute | solution.py:17
  138.7 9.8 %collective-permute-start = (f32[4,128,128]{2,1,0:T(8,128)S(1)}, f32[4,128,128]{2,1,0:T(8,128)S(1)}, u32[]{:S(2)}, u32[]{:S(2)}) collective-permute-start(f32[4,128,128]{2,1,0:T(8,128)S(1)} %multiply_add_fusion.3), channel_id=1, source_target_pairs={{0,16},{16,32},{32,48},{48,64},{64,80},{80,96},{96,112},{112,128},... | collective-permute-start | bytes 786440 | tf_op jit(solution)/shard_map/while/body/eval_jaxpr/ppermute | solution.py:17
  148.6 9.8 %collective-permute-start = (f32[4,128,128]{2,1,0:T(8,128)S(1)}, f32[4,128,128]{2,1,0:T(8,128)S(1)}, u32[]{:S(2)}, u32[]{:S(2)}) collective-permute-start(f32[4,128,128]{2,1,0:T(8,128)S(1)} %multiply_add_fusion.3), channel_id=1, source_target_pairs={{0,16},{16,32},{32,48},{48,64},{64,80},{80,96},{96,112},{112,128},... | collective-permute-start | bytes 786440 | tf_op jit(solution)/shard_map/while/body/eval_jaxpr/ppermute | solution.py:17
  158.5 9.8 %collective-permute-start = (f32[4,128,128]{2,1,0:T(8,128)S(1)}, f32[4,128,128]{2,1,0:T(8,128)S(1)}, u32[]{:S(2)}, u32[]{:S(2)}) collective-permute-start(f32[4,128,128]{2,1,0:T(8,128)S(1)} %multiply_add_fusion.3), channel_id=1, source_target_pairs={{0,16},{16,32},{32,48},{48,64},{64,80},{80,96},{96,112},{112,128},... | collective-permute-start | bytes 786440 | tf_op jit(solution)/shard_map/while/body/eval_jaxpr/ppermute | solution.py:17
  168.4 9.8 %collective-permute-start = (f32[4,128,128]{2,1,0:T(8,128)S(1)}, f32[4,128,128]{2,1,0:T(8,128)S(1)}, u32[]{:S(2)}, u32[]{:S(2)}) collective-permute-start(f32[4,128,128]{2,1,0:T(8,128)S(1)} %multiply_add_fusion.3), channel_id=1, source_target_pairs={{0,16},{16,32},{32,48},{48,64},{64,80},{80,96},{96,112},{112,128},... | collective-permute-start | bytes 786440 | tf_op jit(solution)/shard_map/while/body/eval_jaxpr/ppermute | solution.py:17
  178.3 9.8 %collective-permute-start = (f32[4,128,128]{2,1,0:T(8,128)S(1)}, f32[4,128,128]{2,1,0:T(8,128)S(1)}, u32[]{:S(2)}, u32[]{:S(2)}) collective-permute-start(f32[4,128,128]{2,1,0:T(8,128)S(1)} %multiply_add_fusion.3), channel_id=1, source_target_pairs={{0,16},{16,32},{32,48},{48,64},{64,80},{80,96},{96,112},{112,128},... | collective-permute-start | bytes 786440 | tf_op jit(solution)/shard_map/while/body/eval_jaxpr/ppermute | solution.py:17
  188.2 9.8 %collective-permute-start = (f32[4,128,128]{2,1,0:T(8,128)S(1)}, f32[4,128,128]{2,1,0:T(8,128)S(1)}, u32[]{:S(2)}, u32[]{:S(2)}) collective-permute-start(f32[4,128,128]{2,1,0:T(8,128)S(1)} %multiply_add_fusion.3), channel_id=1, source_target_pairs={{0,16},{16,32},{32,48},{48,64},{64,80},{80,96},{96,112},{112,128},... | collective-permute-start | bytes 786440 | tf_op jit(solution)/shard_map/while/body/eval_jaxpr/ppermute | solution.py:17
  198.1 9.8 %collective-permute-start = (f32[4,128,128]{2,1,0:T(8,128)S(1)}, f32[4,128,128]{2,1,0:T(8,128)S(1)}, u32[]{:S(2)}, u32[]{:S(2)}) collective-permute-start(f32[4,128,128]{2,1,0:T(8,128)S(1)} %multiply_add_fusion.3), channel_id=1, source_target_pairs={{0,16},{16,32},{32,48},{48,64},{64,80},{80,96},{96,112},{112,128},... | collective-permute-start | bytes 786440 | tf_op jit(solution)/shard_map/while/body/eval_jaxpr/ppermute | solution.py:17
  208.0 9.8 %collective-permute-start = (f32[4,128,128]{2,1,0:T(8,128)S(1)}, f32[4,128,128]{2,1,0:T(8,128)S(1)}, u32[]{:S(2)}, u32[]{:S(2)}) collective-permute-start(f32[4,128,128]{2,1,0:T(8,128)S(1)} %multiply_add_fusion.3), channel_id=1, source_target_pairs={{0,16},{16,32},{32,48},{48,64},{64,80},{80,96},{96,112},{112,128},... | collective-permute-start | bytes 786440 | tf_op jit(solution)/shard_map/while/body/eval_jaxpr/ppermute | solution.py:17
  217.9 9.8 %collective-permute-start = (f32[4,128,128]{2,1,0:T(8,128)S(1)}, f32[4,128,128]{2,1,0:T(8,128)S(1)}, u32[]{:S(2)}, u32[]{:S(2)}) collective-permute-start(f32[4,128,128]{2,1,0:T(8,128)S(1)} %multiply_add_fusion.3), channel_id=1, source_target_pairs={{0,16},{16,32},{32,48},{48,64},{64,80},{80,96},{96,112},{112,128},... | collective-permute-start | bytes 786440 | tf_op jit(solution)/shard_map/while/body/eval_jaxpr/ppermute | solution.py:17
  227.8 9.8 %collective-permute-start = (f32[4,128,128]{2,1,0:T(8,128)S(1)}, f32[4,128,128]{2,1,0:T(8,128)S(1)}, u32[]{:S(2)}, u32[]{:S(2)}) collective-permute-start(f32[4,128,128]{2,1,0:T(8,128)S(1)} %multiply_add_fusion.3), channel_id=1, source_target_pairs={{0,16},{16,32},{32,48},{48,64},{64,80},{80,96},{96,112},{112,128},... | collective-permute-start | bytes 786440 | tf_op jit(solution)/shard_map/while/body/eval_jaxpr/ppermute | solution.py:17
  237.7 9.8 %collective-permute-start = (f32[4,128,128]{2,1,0:T(8,128)S(1)}, f32[4,128,128]{2,1,0:T(8,128)S(1)}, u32[]{:S(2)}, u32[]{:S(2)}) collective-permute-start(f32[4,128,128]{2,1,0:T(8,128)S(1)} %multiply_add_fusion.3), channel_id=1, source_target_pairs={{0,16},{16,32},{32,48},{48,64},{64,80},{80,96},{96,112},{112,128},... | collective-permute-start | bytes 786440 | tf_op jit(solution)/shard_map/while/body/eval_jaxpr/ppermute | solution.py:17
  247.5 9.8 %collective-permute-start = (f32[4,128,128]{2,1,0:T(8,128)S(1)}, f32[4,128,128]{2,1,0:T(8,128)S(1)}, u32[]{:S(2)}, u32[]{:S(2)}) collective-permute-start(f32[4,128,128]{2,1,0:T(8,128)S(1)} %multiply_add_fusion.3), channel_id=1, source_target_pairs={{0,16},{16,32},{32,48},{48,64},{64,80},{80,96},{96,112},{112,128},... | collective-permute-start | bytes 786440 | tf_op jit(solution)/shard_map/while/body/eval_jaxpr/ppermute | solution.py:17
  257.4 9.8 %collective-permute-start = (f32[4,128,128]{2,1,0:T(8,128)S(1)}, f32[4,128,128]{2,1,0:T(8,128)S(1)}, u32[]{:S(2)}, u32[]{:S(2)}) collective-permute-start(f32[4,128,128]{2,1,0:T(8,128)S(1)} %multiply_add_fusion.3), channel_id=1, source_target_pairs={{0,16},{16,32},{32,48},{48,64},{64,80},{80,96},{96,112},{112,128},... | collective-permute-start | bytes 786440 | tf_op jit(solution)/shard_map/while/body/eval_jaxpr/ppermute | solution.py:17
  267.3 9.8 %collective-permute-start = (f32[4,128,128]{2,1,0:T(8,128)S(1)}, f32[4,128,128]{2,1,0:T(8,128)S(1)}, u32[]{:S(2)}, u32[]{:S(2)}) collective-permute-start(f32[4,128,128]{2,1,0:T(8,128)S(1)} %multiply_add_fusion.3), channel_id=1, source_target_pairs={{0,16},{16,32},{32,48},{48,64},{64,80},{80,96},{96,112},{112,128},... | collective-permute-start | bytes 786440 | tf_op jit(solution)/shard_map/while/body/eval_jaxpr/ppermute | solution.py:17
  277.2 9.8 %collective-permute-start = (f32[4,128,128]{2,1,0:T(8,128)S(1)}, f32[4,128,128]{2,1,0:T(8,128)S(1)}, u32[]{:S(2)}, u32[]{:S(2)}) collective-permute-start(f32[4,128,128]{2,1,0:T(8,128)S(1)} %multiply_add_fusion.3), channel_id=1, source_target_pairs={{0,16},{16,32},{32,48},{48,64},{64,80},{80,96},{96,112},{112,128},... | collective-permute-start | bytes 786440 | tf_op jit(solution)/shard_map/while/body/eval_jaxpr/ppermute | solution.py:17
  287.1 9.8 %collective-permute-start = (f32[4,128,128]{2,1,0:T(8,128)S(1)}, f32[4,128,128]{2,1,0:T(8,128)S(1)}, u32[]{:S(2)}, u32[]{:S(2)}) collective-permute-start(f32[4,128,128]{2,1,0:T(8,128)S(1)} %multiply_add_fusion.3), channel_id=1, source_target_pairs={{0,16},{16,32},{32,48},{48,64},{64,80},{80,96},{96,112},{112,128},... | collective-permute-start | bytes 786440 | tf_op jit(solution)/shard_map/while/body/eval_jaxpr/ppermute | solution.py:17
  297.0 9.8 %collective-permute-start = (f32[4,128,128]{2,1,0:T(8,128)S(1)}, f32[4,128,128]{2,1,0:T(8,128)S(1)}, u32[]{:S(2)}, u32[]{:S(2)}) collective-permute-start(f32[4,128,128]{2,1,0:T(8,128)S(1)} %multiply_add_fusion.3), channel_id=1, source_target_pairs={{0,16},{16,32},{32,48},{48,64},{64,80},{80,96},{96,112},{112,128},... | collective-permute-start | bytes 786440 | tf_op jit(solution)/shard_map/while/body/eval_jaxpr/ppermute | solution.py:17
  306.9 9.8 %collective-permute-start = (f32[4,128,128]{2,1,0:T(8,128)S(1)}, f32[4,128,128]{2,1,0:T(8,128)S(1)}, u32[]{:S(2)}, u32[]{:S(2)}) collective-permute-start(f32[4,128,128]{2,1,0:T(8,128)S(1)} %multiply_add_fusion.3), channel_id=1, source_target_pairs={{0,16},{16,32},{32,48},{48,64},{64,80},{80,96},{96,112},{112,128},... | collective-permute-start | bytes 786440 | tf_op jit(solution)/shard_map/while/body/eval_jaxpr/ppermute | solution.py:17
  316.8 9.8 %collective-permute-start = (f32[4,128,128]{2,1,0:T(8,128)S(1)}, f32[4,128,128]{2,1,0:T(8,128)S(1)}, u32[]{:S(2)}, u32[]{:S(2)}) collective-permute-start(f32[4,128,128]{2,1,0:T(8,128)S(1)} %multiply_add_fusion.3), channel_id=1, source_target_pairs={{0,16},{16,32},{32,48},{48,64},{64,80},{80,96},{96,112},{112,128},... | collective-permute-start | bytes 786440 | tf_op jit(solution)/shard_map/while/body/eval_jaxpr/ppermute | solution.py:17
  327.4 38.3 %copy-start.3 = (f32[512]{0:T(512)S(1)}, f32[512]{0:T(512)}, u32[]{:S(2)}) copy-start(f32[512]{0:T(512)} %param.18) | copy-start | bytes 6148
Sparse Core Ops, SparseCore 0:
  11.7 64.7 all-gather.2
  79.7 60.1 all-gather.4
where the time goes:
time: 455 us; the launch traced here: 451 us
  waiting for transfers between devices  247 us (54%)
  matrix products  66.5 us (15%)
  starting transfers between devices  59.6 us (13%)
  blocking collectives  37.5 us (8%)
  other arithmetic  15.5 us (3%)
  between operations  14.2 us (3%)
  local copies, waits for them, and re-layouts  7.01 us (2%)
    ppermute x31, waiting for transfers between devices, shifted(): lax.ppermute(value, axis, [(source, source + steps) for source in range(f...  247 us
    ppermute x31, starting transfers between devices, shifted(): lax.ppermute(value, axis, [(source, source + steps) for source in range(f...  59.5 us
    psum x1, blocking collectives, local(): lax.psum(jnp.sum(mixed * mixed, axis=1), 'head') / (QUERY_HEADS * DH)  37.5 us
    dot_general x25, matrix products, soft_update(): jnp.einsum('kgts,ske->kgte', rounded, value_rows, preferred_element_type=...  35 us
    dot_general x25, matrix products, soft_update(): jnp.einsum('tkgd,skd->kgts', queries, key_rows, preferred_element_type=jn...  29.2 us
  transfers between devices with their start and end apart: 33, of which 31 were waited for; matrix products, arithmetic and copies ran while one was open for 3% of the time, Pallas kernels for 0%

commit v1 on v0

--- a/solution.py
+++ b/solution.py
@@ -112,7 +112,9 @@
     entering = lax.fori_loop(0, lax.axis_size("ctx") - 1, advance, jnp.zeros_like(block_state))
     carried = jnp.einsum("thd,hde->the", lifted, entering, precision=lax.Precision.HIGHEST)
     mixed = (local_part + carried).reshape(row_count, width)
-    power = lax.psum(jnp.sum(mixed * mixed, axis=1), "head") / (QUERY_HEADS * DH)
+    power = jnp.sum(lax.all_gather(jnp.sum(mixed * mixed, axis=1), "head"), axis=0) / (
+        QUERY_HEADS * DH
+    )
     linear_out = (mixed * lax.rsqrt(power + EPSILON)[:, None] * norm_gain[None, :]).astype(
         jnp.bfloat16
     )

time: 455 us -> 454 us (level)
    psum x1 -> x0, blocking collectives: 37.5 us -> none  [local(): lax.psum(jnp.sum(mixed * mixed, axis=1), 'head') / (QUERY_HEADS * DH)]
    all_gather x0 -> x1, blocking collectives: none -> 36.4 us  [local(): lax.all_gather(jnp.sum(mixed * mixed, axis=1), 'head')]
where the time goes in v1:
time: 454 us; the launch traced here: 450 us
  waiting for transfers between devices  247 us (54%)
  matrix products  66.5 us (15%)
  starting transfers between devices  59.6 us (13%)
  blocking collectives  36.4 us (8%)
  other arithmetic  15.5 us (3%)
  between operations  14.2 us (3%)
  local copies, waits for them, and re-layouts  7.01 us (2%)
    ppermute x31, waiting for transfers between devices, shifted(): lax.ppermute(value, axis, [(source, source + steps) for source in range(f...  247 us
    ppermute x31, starting transfers between devices, shifted(): lax.ppermute(value, axis, [(source, source + steps) for source in range(f...  59.5 us
    all_gather x1, blocking collectives, local(): lax.all_gather(jnp.sum(mixed * mixed, axis=1), 'head')  36.4 us
    dot_general x25, matrix products, soft_update(): jnp.einsum('kgts,ske->kgte', rounded, value_rows, preferred_element_type=...  35 us
    dot_general x25, matrix products, soft_update(): jnp.einsum('tkgd,skd->kgts', queries, key_rows, preferred_element_type=jn...  29.2 us
  transfers between devices with their start and end apart: 33, of which 31 were waited for; matrix products, arithmetic and copies ran while one was open for 3% of the time, Pallas kernels for 0%

profile of v1, /device:TPU:6, one launch (start us, length us, event | category | flops | bytes accessed | tf_op | source)
XLA Modules:
  0.0 450.1 jit_solution(5125077079905695359)
XLA Ops:
  16.4 310.2 %while.9 = (s32[]{:T(128)}, f32[4,128,128]{2,1,0:T(8,128)S(1)}, f32[4]{0:T(128)S(1)}, f32[4,128,128]{2,1,0:T(8,128)S(1)}, s32[]{:T(128)}) while((s32[]{:T(128)}, f32[4,128,128]{2,1,0:T(8,128)S(1)}, f32[4]{0:T(128)S(1)}, f32[4,128,128]{2,1,0:T(8,128)S(1)}, s32[]{:T(128)}) %tuple.86), condition=%wide.region_3.4_spmd, body=%wide.region_2.3_spmd.sunk | while | flops 131074 | bytes 1835125 | solution.py:112
  18.5 7.9 %collective-permute-done = f32[4,128,128]{2,1,0:T(8,128)S(1)} collective-permute-done((f32[4,128,128]{2,1,0:T(8,128)S(1)}, f32[4,128,128]{2,1,0:T(8,128)S(1)}, u32[]{:S(2)}, u32[]{:S(2)}) %collective-permute-start) | collective-permute-done | bytes 262176 | tf_op jit(solution)/shard_map/while/body/eval_jaxpr/ppermute | solution.py:17
  26.4 1.9 collective-permute-start
  28.4 7.9 %collective-permute-done = f32[4,128,128]{2,1,0:T(8,128)S(1)} collective-permute-done((f32[4,128,128]{2,1,0:T(8,128)S(1)}, f32[4,128,128]{2,1,0:T(8,128)S(1)}, u32[]{:S(2)}, u32[]{:S(2)}) %collective-permute-start) | collective-permute-done | bytes 262176 | tf_op jit(solution)/shard_map/while/body/eval_jaxpr/ppermute | solution.py:17
  38.3 8.0 %collective-permute-done = f32[4,128,128]{2,1,0:T(8,128)S(1)} collective-permute-done((f32[4,128,128]{2,1,0:T(8,128)S(1)}, f32[4,128,128]{2,1,0:T(8,128)S(1)}, u32[]{:S(2)}, u32[]{:S(2)}) %collective-permute-start) | collective-permute-done | bytes 262176 | tf_op jit(solution)/shard_map/while/body/eval_jaxpr/ppermute | solution.py:17
  46.4 1.9 collective-permute-start
  48.3 7.9 %collective-permute-done = f32[4,128,128]{2,1,0:T(8,128)S(1)} collective-permute-done((f32[4,128,128]{2,1,0:T(8,128)S(1)}, f32[4,128,128]{2,1,0:T(8,128)S(1)}, u32[]{:S(2)}, u32[]{:S(2)}) %collective-permute-start) | collective-permute-done | bytes 262176 | tf_op jit(solution)/shard_map/while/body/eval_jaxpr/ppermute | solution.py:17
  56.3 1.9 collective-permute-start
  58.2 8.4 %collective-permute-done = f32[4,128,128]{2,1,0:T(8,128)S(1)} collective-permute-done((f32[4,128,128]{2,1,0:T(8,128)S(1)}, f32[4,128,128]{2,1,0:T(8,128)S(1)}, u32[]{:S(2)}, u32[]{:S(2)}) %collective-permute-start) | collective-permute-done | bytes 262176 | tf_op jit(solution)/shard_map/while/body/eval_jaxpr/ppermute | solution.py:17
  68.6 8.7 %collective-permute-done = f32[4,128,128]{2,1,0:T(8,128)S(1)} collective-permute-done((f32[4,128,128]{2,1,0:T(8,128)S(1)}, f32[4,128,128]{2,1,0:T(8,128)S(1)}, u32[]{:S(2)}, u32[]{:S(2)}) %collective-permute-start) | collective-permute-done | bytes 262176 | tf_op jit(solution)/shard_map/while/body/eval_jaxpr/ppermute | solution.py:17
  79.4 7.9 %collective-permute-done = f32[4,128,128]{2,1,0:T(8,128)S(1)} collective-permute-done((f32[4,128,128]{2,1,0:T(8,128)S(1)}, f32[4,128,128]{2,1,0:T(8,128)S(1)}, u32[]{:S(2)}, u32[]{:S(2)}) %collective-permute-start) | collective-permute-done | bytes 262176 | tf_op jit(solution)/shard_map/while/body/eval_jaxpr/ppermute | solution.py:17
  87.4 1.9 collective-permute-start
  89.3 7.9 %collective-permute-done = f32[4,128,128]{2,1,0:T(8,128)S(1)} collective-permute-done((f32[4,128,128]{2,1,0:T(8,128)S(1)}, f32[4,128,128]{2,1,0:T(8,128)S(1)}, u32[]{:S(2)}, u32[]{:S(2)}) %collective-permute-start) | collective-permute-done | bytes 262176 | tf_op jit(solution)/shard_map/while/body/eval_jaxpr/ppermute | solution.py:17
  99.2 8.3 %collective-permute-done = f32[4,128,128]{2,1,0:T(8,128)S(1)} collective-permute-done((f32[4,128,128]{2,1,0:T(8,128)S(1)}, f32[4,128,128]{2,1,0:T(8,128)S(1)}, u32[]{:S(2)}, u32[]{:S(2)}) %collective-permute-start) | collective-permute-done | bytes 262176 | tf_op jit(solution)/shard_map/while/body/eval_jaxpr/ppermute | solution.py:17
  107.6 1.9 collective-permute-start
  109.5 7.9 %collective-permute-done = f32[4,128,128]{2,1,0:T(8,128)S(1)} collective-permute-done((f32[4,128,128]{2,1,0:T(8,128)S(1)}, f32[4,128,128]{2,1,0:T(8,128)S(1)}, u32[]{:S(2)}, u32[]{:S(2)}) %collective-permute-start) | collective-permute-done | bytes 262176 | tf_op jit(solution)/shard_map/while/body/eval_jaxpr/ppermute | solution.py:17
  119.4 7.9 %collective-permute-done = f32[4,128,128]{2,1,0:T(8,128)S(1)} collective-permute-done((f32[4,128,128]{2,1,0:T(8,128)S(1)}, f32[4,128,128]{2,1,0:T(8,128)S(1)}, u32[]{:S(2)}, u32[]{:S(2)}) %collective-permute-start) | collective-permute-done | bytes 262176 | tf_op jit(solution)/shard_map/while/body/eval_jaxpr/ppermute | solution.py:17
  129.3 9.3 %collective-permute-done = f32[4,128,128]{2,1,0:T(8,128)S(1)} collective-permute-done((f32[4,128,128]{2,1,0:T(8,128)S(1)}, f32[4,128,128]{2,1,0:T(8,128)S(1)}, u32[]{:S(2)}, u32[]{:S(2)}) %collective-permute-start) | collective-permute-done | bytes 262176 | tf_op jit(solution)/shard_map/while/body/eval_jaxpr/ppermute | solution.py:17
  140.6 7.9 %collective-permute-done = f32[4,128,128]{2,1,0:T(8,128)S(1)} collective-permute-done((f32[4,128,128]{2,1,0:T(8,128)S(1)}, f32[4,128,128]{2,1,0:T(8,128)S(1)}, u32[]{:S(2)}, u32[]{:S(2)}) %collective-permute-start) | collective-permute-done | bytes 262176 | tf_op jit(solution)/shard_map/while/body/eval_jaxpr/ppermute | solution.py:17
  150.5 7.9 %collective-permute-done = f32[4,128,128]{2,1,0:T(8,128)S(1)} collective-permute-done((f32[4,128,128]{2,1,0:T(8,128)S(1)}, f32[4,128,128]{2,1,0:T(8,128)S(1)}, u32[]{:S(2)}, u32[]{:S(2)}) %collective-permute-start) | collective-permute-done | bytes 262176 | tf_op jit(solution)/shard_map/while/body/eval_jaxpr/ppermute | solution.py:17
  160.4 7.9 %collective-permute-done = f32[4,128,128]{2,1,0:T(8,128)S(1)} collective-permute-done((f32[4,128,128]{2,1,0:T(8,128)S(1)}, f32[4,128,128]{2,1,0:T(8,128)S(1)}, u32[]{:S(2)}, u32[]{:S(2)}) %collective-permute-start) | collective-permute-done | bytes 262176 | tf_op jit(solution)/shard_map/while/body/eval_jaxpr/ppermute | solution.py:17
  170.3 7.9 %collective-permute-done = f32[4,128,128]{2,1,0:T(8,128)S(1)} collective-permute-done((f32[4,128,128]{2,1,0:T(8,128)S(1)}, f32[4,128,128]{2,1,0:T(8,128)S(1)}, u32[]{:S(2)}, u32[]{:S(2)}) %collective-permute-start) | collective-permute-done | bytes 262176 | tf_op jit(solution)/shard_map/while/body/eval_jaxpr/ppermute | solution.py:17
  180.2 7.9 %collective-permute-done = f32[4,128,128]{2,1,0:T(8,128)S(1)} collective-permute-done((f32[4,128,128]{2,1,0:T(8,128)S(1)}, f32[4,128,128]{2,1,0:T(8,128)S(1)}, u32[]{:S(2)}, u32[]{:S(2)}) %collective-permute-start) | collective-permute-done | bytes 262176 | tf_op jit(solution)/shard_map/while/body/eval_jaxpr/ppermute | solution.py:17
  190.1 7.9 %collective-permute-done = f32[4,128,128]{2,1,0:T(8,128)S(1)} collective-permute-done((f32[4,128,128]{2,1,0:T(8,128)S(1)}, f32[4,128,128]{2,1,0:T(8,128)S(1)}, u32[]{:S(2)}, u32[]{:S(2)}) %collective-permute-start) | collective-permute-done | bytes 262176 | tf_op jit(solution)/shard_map/while/body/eval_jaxpr/ppermute | solution.py:17
  200.0 7.9 %collective-permute-done = f32[4,128,128]{2,1,0:T(8,128)S(1)} collective-permute-done((f32[4,128,128]{2,1,0:T(8,128)S(1)}, f32[4,128,128]{2,1,0:T(8,128)S(1)}, u32[]{:S(2)}, u32[]{:S(2)}) %collective-permute-start) | collective-permute-done | bytes 262176 | tf_op jit(solution)/shard_map/while/body/eval_jaxpr/ppermute | solution.py:17
  209.9 7.9 %collective-permute-done = f32[4,128,128]{2,1,0:T(8,128)S(1)} collective-permute-done((f32[4,128,128]{2,1,0:T(8,128)S(1)}, f32[4,128,128]{2,1,0:T(8,128)S(1)}, u32[]{:S(2)}, u32[]{:S(2)}) %collective-permute-start) | collective-permute-done | bytes 262176 | tf_op jit(solution)/shard_map/while/body/eval_jaxpr/ppermute | solution.py:17
  219.8 7.9 %collective-permute-done = f32[4,128,128]{2,1,0:T(8,128)S(1)} collective-permute-done((f32[4,128,128]{2,1,0:T(8,128)S(1)}, f32[4,128,128]{2,1,0:T(8,128)S(1)}, u32[]{:S(2)}, u32[]{:S(2)}) %collective-permute-start) | collective-permute-done | bytes 262176 | tf_op jit(solution)/shard_map/while/body/eval_jaxpr/ppermute | solution.py:17
  229.7 7.9 %collective-permute-done = f32[4,128,128]{2,1,0:T(8,128)S(1)} collective-permute-done((f32[4,128,128]{2,1,0:T(8,128)S(1)}, f32[4,128,128]{2,1,0:T(8,128)S(1)}, u32[]{:S(2)}, u32[]{:S(2)}) %collective-permute-start) | collective-permute-done | bytes 262176 | tf_op jit(solution)/shard_map/while/body/eval_jaxpr/ppermute | solution.py:17
  239.6 7.9 %collective-permute-done = f32[4,128,128]{2,1,0:T(8,128)S(1)} collective-permute-done((f32[4,128,128]{2,1,0:T(8,128)S(1)}, f32[4,128,128]{2,1,0:T(8,128)S(1)}, u32[]{:S(2)}, u32[]{:S(2)}) %collective-permute-start) | collective-permute-done | bytes 262176 | tf_op jit(solution)/shard_map/while/body/eval_jaxpr/ppermute | solution.py:17
  249.5 7.9 %collective-permute-done = f32[4,128,128]{2,1,0:T(8,128)S(1)} collective-permute-done((f32[4,128,128]{2,1,0:T(8,128)S(1)}, f32[4,128,128]{2,1,0:T(8,128)S(1)}, u32[]{:S(2)}, u32[]{:S(2)}) %collective-permute-start) | collective-permute-done | bytes 262176 | tf_op jit(solution)/shard_map/while/body/eval_jaxpr/ppermute | solution.py:17
  259.4 7.9 %collective-permute-done = f32[4,128,128]{2,1,0:T(8,128)S(1)} collective-permute-done((f32[4,128,128]{2,1,0:T(8,128)S(1)}, f32[4,128,128]{2,1,0:T(8,128)S(1)}, u32[]{:S(2)}, u32[]{:S(2)}) %collective-permute-start) | collective-permute-done | bytes 262176 | tf_op jit(solution)/shard_map/while/body/eval_jaxpr/ppermute | solution.py:17
  269.3 7.9 %collective-permute-done = f32[4,128,128]{2,1,0:T(8,128)S(1)} collective-permute-done((f32[4,128,128]{2,1,0:T(8,128)S(1)}, f32[4,128,128]{2,1,0:T(8,128)S(1)}, u32[]{:S(2)}, u32[]{:S(2)}) %collective-permute-start) | collective-permute-done | bytes 262176 | tf_op jit(solution)/shard_map/while/body/eval_jaxpr/ppermute | solution.py:17
  279.2 7.9 %collective-permute-done = f32[4,128,128]{2,1,0:T(8,128)S(1)} collective-permute-done((f32[4,128,128]{2,1,0:T(8,128)S(1)}, f32[4,128,128]{2,1,0:T(8,128)S(1)}, u32[]{:S(2)}, u32[]{:S(2)}) %collective-permute-start) | collective-permute-done | bytes 262176 | tf_op jit(solution)/shard_map/while/body/eval_jaxpr/ppermute | solution.py:17
  289.1 7.9 %collective-permute-done = f32[4,128,128]{2,1,0:T(8,128)S(1)} collective-permute-done((f32[4,128,128]{2,1,0:T(8,128)S(1)}, f32[4,128,128]{2,1,0:T(8,128)S(1)}, u32[]{:S(2)}, u32[]{:S(2)}) %collective-permute-start) | collective-permute-done | bytes 262176 | tf_op jit(solution)/shard_map/while/body/eval_jaxpr/ppermute | solution.py:17
  299.0 7.9 %collective-permute-done = f32[4,128,128]{2,1,0:T(8,128)S(1)} collective-permute-done((f32[4,128,128]{2,1,0:T(8,128)S(1)}, f32[4,128,128]{2,1,0:T(8,128)S(1)}, u32[]{:S(2)}, u32[]{:S(2)}) %collective-permute-start) | collective-permute-done | bytes 262176 | tf_op jit(solution)/shard_map/while/body/eval_jaxpr/ppermute | solution.py:17
  308.9 7.9 %collective-permute-done = f32[4,128,128]{2,1,0:T(8,128)S(1)} collective-permute-done((f32[4,128,128]{2,1,0:T(8,128)S(1)}, f32[4,128,128]{2,1,0:T(8,128)S(1)}, u32[]{:S(2)}, u32[]{:S(2)}) %collective-permute-start) | collective-permute-done | bytes 262176 | tf_op jit(solution)/shard_map/while/body/eval_jaxpr/ppermute | solution.py:17
  318.8 7.9 %collective-permute-done = f32[4,128,128]{2,1,0:T(8,128)S(1)} collective-permute-done((f32[4,128,128]{2,1,0:T(8,128)S(1)}, f32[4,128,128]{2,1,0:T(8,128)S(1)}, u32[]{:S(2)}, u32[]{:S(2)}) %collective-permute-start) | collective-permute-done | bytes 262176 | tf_op jit(solution)/shard_map/while/body/eval_jaxpr/ppermute | solution.py:17
  328.2 36.4 %all-gather.1 = f32[16,1,256]{2,1,0:T(1,128)S(1)} all-gather(f32[1,1,256]{2,1,0:T(1,128)S(1)} %bitcast.124), channel_id=2, replica_groups=mesh['ctx'=32,'head'=16] {'head'}, dimensions={0}, use_global_device_ids=true | all-gather | bytes 17408 | tf_op jit(solution)/shard_map/all_gather | solution.py:115
  365.6 76.8 %while.36 = (s32[]{:T(128)}, f32[4,256]{1,0:T(4,128)S(1)}, f32[4,256]{1,0:T(4,128)S(1)}, f32[4,256,128]{2,1,0:T(8,128)S(1)}, s32[]{:T(128)}, /*index=5*/bf16[819...) while((s32[]{:T(128)}, f32[4,256]{1,0:T(4,128)S(1)}, ...), condition=%wide.region_11.12_spmd.clone, body=%wide.region_6.11_spmd.clone.sunk | while | flops 137431552 | bytes 4922689 | solution.py:74
  365.6 3.0 conditional.3
  368.7 3.0 conditional.3
  371.7 3.0 conditional.3
  374.8 3.0 conditional.3
  377.8 3.0 conditional.3
  380.9 3.0 conditional.3
  383.9 3.0 conditional.3
  387.0 3.0 conditional.3
  390.0 3.0 conditional.3
  393.1 3.0 conditional.3
  396.2 3.0 conditional.3
  399.2 3.0 conditional.3
  402.3 3.0 conditional.3
  405.3 3.0 conditional.3
  408.4 3.0 conditional.3
  411.4 3.0 conditional.3
  414.5 3.0 conditional.3
  417.6 3.0 conditional.3
  420.6 3.0 conditional.3
  423.7 3.0 conditional.3
  426.7 3.0 conditional.3
  429.8 3.0 conditional.3
  432.8 3.0 conditional.3
  435.9 3.0 conditional.3
  439.0 3.0 conditional.3
  (341 shorter events, 139.1 us)
Async XLA Ops:
  7.2 1.0 copy-start
  7.2 8.2 %copy-start.1 = (bf16[256,512]{1,0:T(8,128)(2,1)S(1)}, bf16[256,512]{1,0:T(8,128)(2,1)}, u32[]{:S(2)}) copy-start(bf16[256,512]{1,0:T(8,128)(2,1)} %param.14) | copy-start | bytes 786436
  7.2 9.0 %copy-start.2 = (bf16[256,512]{1,0:T(8,128)(2,1)S(1)}, bf16[256,512]{1,0:T(8,128)(2,1)}, u32[]{:S(2)}) copy-start(bf16[256,512]{1,0:T(8,128)(2,1)} %param.16) | copy-start | bytes 786436
  7.2 358.3 %all-gather.5.cloned.1.call-start = ((), (), s32[]{:S(2)}) async-start(), calls=%async_computation | async-start | bytes 2162688 | tf_op jit(solution)/shard_map/all_gather | solution.py:158
  8.9 356.6 %all-gather.7.cloned.1.call-start = ((), (), s32[]{:S(2)}) async-start(), calls=%async_computation.1 | async-start | bytes 2162688 | tf_op jit(solution)/shard_map/all_gather | solution.py:159
  16.5 9.8 %collective-permute-start = (f32[4,128,128]{2,1,0:T(8,128)S(1)}, f32[4,128,128]{2,1,0:T(8,128)S(1)}, u32[]{:S(2)}, u32[]{:S(2)}) collective-permute-start(f32[4,128,128]{2,1,0:T(8,128)S(1)} %multiply_add_fusion.3), channel_id=1, source_target_pairs={{0,16},{16,32},{32,48},{48,64},{64,80},{80,96},{96,112},{112,128},... | collective-permute-start | bytes 786440 | tf_op jit(solution)/shard_map/while/body/eval_jaxpr/ppermute | solution.py:17
  26.4 9.8 %collective-permute-start = (f32[4,128,128]{2,1,0:T(8,128)S(1)}, f32[4,128,128]{2,1,0:T(8,128)S(1)}, u32[]{:S(2)}, u32[]{:S(2)}) collective-permute-start(f32[4,128,128]{2,1,0:T(8,128)S(1)} %multiply_add_fusion.3), channel_id=1, source_target_pairs={{0,16},{16,32},{32,48},{48,64},{64,80},{80,96},{96,112},{112,128},... | collective-permute-start | bytes 786440 | tf_op jit(solution)/shard_map/while/body/eval_jaxpr/ppermute | solution.py:17
  36.3 10.0 %collective-permute-start = (f32[4,128,128]{2,1,0:T(8,128)S(1)}, f32[4,128,128]{2,1,0:T(8,128)S(1)}, u32[]{:S(2)}, u32[]{:S(2)}) collective-permute-start(f32[4,128,128]{2,1,0:T(8,128)S(1)} %multiply_add_fusion.3), channel_id=1, source_target_pairs={{0,16},{16,32},{32,48},{48,64},{64,80},{80,96},{96,112},{112,128},... | collective-permute-start | bytes 786440 | tf_op jit(solution)/shard_map/while/body/eval_jaxpr/ppermute | solution.py:17
  46.4 9.8 %collective-permute-start = (f32[4,128,128]{2,1,0:T(8,128)S(1)}, f32[4,128,128]{2,1,0:T(8,128)S(1)}, u32[]{:S(2)}, u32[]{:S(2)}) collective-permute-start(f32[4,128,128]{2,1,0:T(8,128)S(1)} %multiply_add_fusion.3), channel_id=1, source_target_pairs={{0,16},{16,32},{32,48},{48,64},{64,80},{80,96},{96,112},{112,128},... | collective-permute-start | bytes 786440 | tf_op jit(solution)/shard_map/while/body/eval_jaxpr/ppermute | solution.py:17
  56.3 10.3 %collective-permute-start = (f32[4,128,128]{2,1,0:T(8,128)S(1)}, f32[4,128,128]{2,1,0:T(8,128)S(1)}, u32[]{:S(2)}, u32[]{:S(2)}) collective-permute-start(f32[4,128,128]{2,1,0:T(8,128)S(1)} %multiply_add_fusion.3), channel_id=1, source_target_pairs={{0,16},{16,32},{32,48},{48,64},{64,80},{80,96},{96,112},{112,128},... | collective-permute-start | bytes 786440 | tf_op jit(solution)/shard_map/while/body/eval_jaxpr/ppermute | solution.py:17
  66.7 10.7 %collective-permute-start = (f32[4,128,128]{2,1,0:T(8,128)S(1)}, f32[4,128,128]{2,1,0:T(8,128)S(1)}, u32[]{:S(2)}, u32[]{:S(2)}) collective-permute-start(f32[4,128,128]{2,1,0:T(8,128)S(1)} %multiply_add_fusion.3), channel_id=1, source_target_pairs={{0,16},{16,32},{32,48},{48,64},{64,80},{80,96},{96,112},{112,128},... | collective-permute-start | bytes 786440 | tf_op jit(solution)/shard_map/while/body/eval_jaxpr/ppermute | solution.py:17
  77.5 9.8 %collective-permute-start = (f32[4,128,128]{2,1,0:T(8,128)S(1)}, f32[4,128,128]{2,1,0:T(8,128)S(1)}, u32[]{:S(2)}, u32[]{:S(2)}) collective-permute-start(f32[4,128,128]{2,1,0:T(8,128)S(1)} %multiply_add_fusion.3), channel_id=1, source_target_pairs={{0,16},{16,32},{32,48},{48,64},{64,80},{80,96},{96,112},{112,128},... | collective-permute-start | bytes 786440 | tf_op jit(solution)/shard_map/while/body/eval_jaxpr/ppermute | solution.py:17
  87.4 9.8 %collective-permute-start = (f32[4,128,128]{2,1,0:T(8,128)S(1)}, f32[4,128,128]{2,1,0:T(8,128)S(1)}, u32[]{:S(2)}, u32[]{:S(2)}) collective-permute-start(f32[4,128,128]{2,1,0:T(8,128)S(1)} %multiply_add_fusion.3), channel_id=1, source_target_pairs={{0,16},{16,32},{32,48},{48,64},{64,80},{80,96},{96,112},{112,128},... | collective-permute-start | bytes 786440 | tf_op jit(solution)/shard_map/while/body/eval_jaxpr/ppermute | solution.py:17
  97.3 10.2 %collective-permute-start = (f32[4,128,128]{2,1,0:T(8,128)S(1)}, f32[4,128,128]{2,1,0:T(8,128)S(1)}, u32[]{:S(2)}, u32[]{:S(2)}) collective-permute-start(f32[4,128,128]{2,1,0:T(8,128)S(1)} %multiply_add_fusion.3), channel_id=1, source_target_pairs={{0,16},{16,32},{32,48},{48,64},{64,80},{80,96},{96,112},{112,128},... | collective-permute-start | bytes 786440 | tf_op jit(solution)/shard_map/while/body/eval_jaxpr/ppermute | solution.py:17
  107.6 9.8 %collective-permute-start = (f32[4,128,128]{2,1,0:T(8,128)S(1)}, f32[4,128,128]{2,1,0:T(8,128)S(1)}, u32[]{:S(2)}, u32[]{:S(2)}) collective-permute-start(f32[4,128,128]{2,1,0:T(8,128)S(1)} %multiply_add_fusion.3), channel_id=1, source_target_pairs={{0,16},{16,32},{32,48},{48,64},{64,80},{80,96},{96,112},{112,128},... | collective-permute-start | bytes 786440 | tf_op jit(solution)/shard_map/while/body/eval_jaxpr/ppermute | solution.py:17
  117.5 9.8 %collective-permute-start = (f32[4,128,128]{2,1,0:T(8,128)S(1)}, f32[4,128,128]{2,1,0:T(8,128)S(1)}, u32[]{:S(2)}, u32[]{:S(2)}) collective-permute-start(f32[4,128,128]{2,1,0:T(8,128)S(1)} %multiply_add_fusion.3), channel_id=1, source_target_pairs={{0,16},{16,32},{32,48},{48,64},{64,80},{80,96},{96,112},{112,128},... | collective-permute-start | bytes 786440 | tf_op jit(solution)/shard_map/while/body/eval_jaxpr/ppermute | solution.py:17
  127.4 11.2 %collective-permute-start = (f32[4,128,128]{2,1,0:T(8,128)S(1)}, f32[4,128,128]{2,1,0:T(8,128)S(1)}, u32[]{:S(2)}, u32[]{:S(2)}) collective-permute-start(f32[4,128,128]{2,1,0:T(8,128)S(1)} %multiply_add_fusion.3), channel_id=1, source_target_pairs={{0,16},{16,32},{32,48},{48,64},{64,80},{80,96},{96,112},{112,128},... | collective-permute-start | bytes 786440 | tf_op jit(solution)/shard_map/while/body/eval_jaxpr/ppermute | solution.py:17
  138.7 9.8 %collective-permute-start = (f32[4,128,128]{2,1,0:T(8,128)S(1)}, f32[4,128,128]{2,1,0:T(8,128)S(1)}, u32[]{:S(2)}, u32[]{:S(2)}) collective-permute-start(f32[4,128,128]{2,1,0:T(8,128)S(1)} %multiply_add_fusion.3), channel_id=1, source_target_pairs={{0,16},{16,32},{32,48},{48,64},{64,80},{80,96},{96,112},{112,128},... | collective-permute-start | bytes 786440 | tf_op jit(solution)/shard_map/while/body/eval_jaxpr/ppermute | solution.py:17
  148.6 9.8 %collective-permute-start = (f32[4,128,128]{2,1,0:T(8,128)S(1)}, f32[4,128,128]{2,1,0:T(8,128)S(1)}, u32[]{:S(2)}, u32[]{:S(2)}) collective-permute-start(f32[4,128,128]{2,1,0:T(8,128)S(1)} %multiply_add_fusion.3), channel_id=1, source_target_pairs={{0,16},{16,32},{32,48},{48,64},{64,80},{80,96},{96,112},{112,128},... | collective-permute-start | bytes 786440 | tf_op jit(solution)/shard_map/while/body/eval_jaxpr/ppermute | solution.py:17
  158.5 9.8 %collective-permute-start = (f32[4,128,128]{2,1,0:T(8,128)S(1)}, f32[4,128,128]{2,1,0:T(8,128)S(1)}, u32[]{:S(2)}, u32[]{:S(2)}) collective-permute-start(f32[4,128,128]{2,1,0:T(8,128)S(1)} %multiply_add_fusion.3), channel_id=1, source_target_pairs={{0,16},{16,32},{32,48},{48,64},{64,80},{80,96},{96,112},{112,128},... | collective-permute-start | bytes 786440 | tf_op jit(solution)/shard_map/while/body/eval_jaxpr/ppermute | solution.py:17
  168.4 9.8 %collective-permute-start = (f32[4,128,128]{2,1,0:T(8,128)S(1)}, f32[4,128,128]{2,1,0:T(8,128)S(1)}, u32[]{:S(2)}, u32[]{:S(2)}) collective-permute-start(f32[4,128,128]{2,1,0:T(8,128)S(1)} %multiply_add_fusion.3), channel_id=1, source_target_pairs={{0,16},{16,32},{32,48},{48,64},{64,80},{80,96},{96,112},{112,128},... | collective-permute-start | bytes 786440 | tf_op jit(solution)/shard_map/while/body/eval_jaxpr/ppermute | solution.py:17
  178.3 9.8 %collective-permute-start = (f32[4,128,128]{2,1,0:T(8,128)S(1)}, f32[4,128,128]{2,1,0:T(8,128)S(1)}, u32[]{:S(2)}, u32[]{:S(2)}) collective-permute-start(f32[4,128,128]{2,1,0:T(8,128)S(1)} %multiply_add_fusion.3), channel_id=1, source_target_pairs={{0,16},{16,32},{32,48},{48,64},{64,80},{80,96},{96,112},{112,128},... | collective-permute-start | bytes 786440 | tf_op jit(solution)/shard_map/while/body/eval_jaxpr/ppermute | solution.py:17
  188.2 9.8 %collective-permute-start = (f32[4,128,128]{2,1,0:T(8,128)S(1)}, f32[4,128,128]{2,1,0:T(8,128)S(1)}, u32[]{:S(2)}, u32[]{:S(2)}) collective-permute-start(f32[4,128,128]{2,1,0:T(8,128)S(1)} %multiply_add_fusion.3), channel_id=1, source_target_pairs={{0,16},{16,32},{32,48},{48,64},{64,80},{80,96},{96,112},{112,128},... | collective-permute-start | bytes 786440 | tf_op jit(solution)/shard_map/while/body/eval_jaxpr/ppermute | solution.py:17
  198.1 9.8 %collective-permute-start = (f32[4,128,128]{2,1,0:T(8,128)S(1)}, f32[4,128,128]{2,1,0:T(8,128)S(1)}, u32[]{:S(2)}, u32[]{:S(2)}) collective-permute-start(f32[4,128,128]{2,1,0:T(8,128)S(1)} %multiply_add_fusion.3), channel_id=1, source_target_pairs={{0,16},{16,32},{32,48},{48,64},{64,80},{80,96},{96,112},{112,128},... | collective-permute-start | bytes 786440 | tf_op jit(solution)/shard_map/while/body/eval_jaxpr/ppermute | solution.py:17
  208.0 9.8 %collective-permute-start = (f32[4,128,128]{2,1,0:T(8,128)S(1)}, f32[4,128,128]{2,1,0:T(8,128)S(1)}, u32[]{:S(2)}, u32[]{:S(2)}) collective-permute-start(f32[4,128,128]{2,1,0:T(8,128)S(1)} %multiply_add_fusion.3), channel_id=1, source_target_pairs={{0,16},{16,32},{32,48},{48,64},{64,80},{80,96},{96,112},{112,128},... | collective-permute-start | bytes 786440 | tf_op jit(solution)/shard_map/while/body/eval_jaxpr/ppermute | solution.py:17
  217.9 9.8 %collective-permute-start = (f32[4,128,128]{2,1,0:T(8,128)S(1)}, f32[4,128,128]{2,1,0:T(8,128)S(1)}, u32[]{:S(2)}, u32[]{:S(2)}) collective-permute-start(f32[4,128,128]{2,1,0:T(8,128)S(1)} %multiply_add_fusion.3), channel_id=1, source_target_pairs={{0,16},{16,32},{32,48},{48,64},{64,80},{80,96},{96,112},{112,128},... | collective-permute-start | bytes 786440 | tf_op jit(solution)/shard_map/while/body/eval_jaxpr/ppermute | solution.py:17
  227.8 9.8 %collective-permute-start = (f32[4,128,128]{2,1,0:T(8,128)S(1)}, f32[4,128,128]{2,1,0:T(8,128)S(1)}, u32[]{:S(2)}, u32[]{:S(2)}) collective-permute-start(f32[4,128,128]{2,1,0:T(8,128)S(1)} %multiply_add_fusion.3), channel_id=1, source_target_pairs={{0,16},{16,32},{32,48},{48,64},{64,80},{80,96},{96,112},{112,128},... | collective-permute-start | bytes 786440 | tf_op jit(solution)/shard_map/while/body/eval_jaxpr/ppermute | solution.py:17
  237.7 9.8 %collective-permute-start = (f32[4,128,128]{2,1,0:T(8,128)S(1)}, f32[4,128,128]{2,1,0:T(8,128)S(1)}, u32[]{:S(2)}, u32[]{:S(2)}) collective-permute-start(f32[4,128,128]{2,1,0:T(8,128)S(1)} %multiply_add_fusion.3), channel_id=1, source_target_pairs={{0,16},{16,32},{32,48},{48,64},{64,80},{80,96},{96,112},{112,128},... | collective-permute-start | bytes 786440 | tf_op jit(solution)/shard_map/while/body/eval_jaxpr/ppermute | solution.py:17
  247.5 9.8 %collective-permute-start = (f32[4,128,128]{2,1,0:T(8,128)S(1)}, f32[4,128,128]{2,1,0:T(8,128)S(1)}, u32[]{:S(2)}, u32[]{:S(2)}) collective-permute-start(f32[4,128,128]{2,1,0:T(8,128)S(1)} %multiply_add_fusion.3), channel_id=1, source_target_pairs={{0,16},{16,32},{32,48},{48,64},{64,80},{80,96},{96,112},{112,128},... | collective-permute-start | bytes 786440 | tf_op jit(solution)/shard_map/while/body/eval_jaxpr/ppermute | solution.py:17
  257.4 9.8 %collective-permute-start = (f32[4,128,128]{2,1,0:T(8,128)S(1)}, f32[4,128,128]{2,1,0:T(8,128)S(1)}, u32[]{:S(2)}, u32[]{:S(2)}) collective-permute-start(f32[4,128,128]{2,1,0:T(8,128)S(1)} %multiply_add_fusion.3), channel_id=1, source_target_pairs={{0,16},{16,32},{32,48},{48,64},{64,80},{80,96},{96,112},{112,128},... | collective-permute-start | bytes 786440 | tf_op jit(solution)/shard_map/while/body/eval_jaxpr/ppermute | solution.py:17
  267.3 9.8 %collective-permute-start = (f32[4,128,128]{2,1,0:T(8,128)S(1)}, f32[4,128,128]{2,1,0:T(8,128)S(1)}, u32[]{:S(2)}, u32[]{:S(2)}) collective-permute-start(f32[4,128,128]{2,1,0:T(8,128)S(1)} %multiply_add_fusion.3), channel_id=1, source_target_pairs={{0,16},{16,32},{32,48},{48,64},{64,80},{80,96},{96,112},{112,128},... | collective-permute-start | bytes 786440 | tf_op jit(solution)/shard_map/while/body/eval_jaxpr/ppermute | solution.py:17
  277.2 9.8 %collective-permute-start = (f32[4,128,128]{2,1,0:T(8,128)S(1)}, f32[4,128,128]{2,1,0:T(8,128)S(1)}, u32[]{:S(2)}, u32[]{:S(2)}) collective-permute-start(f32[4,128,128]{2,1,0:T(8,128)S(1)} %multiply_add_fusion.3), channel_id=1, source_target_pairs={{0,16},{16,32},{32,48},{48,64},{64,80},{80,96},{96,112},{112,128},... | collective-permute-start | bytes 786440 | tf_op jit(solution)/shard_map/while/body/eval_jaxpr/ppermute | solution.py:17
  287.1 9.8 %collective-permute-start = (f32[4,128,128]{2,1,0:T(8,128)S(1)}, f32[4,128,128]{2,1,0:T(8,128)S(1)}, u32[]{:S(2)}, u32[]{:S(2)}) collective-permute-start(f32[4,128,128]{2,1,0:T(8,128)S(1)} %multiply_add_fusion.3), channel_id=1, source_target_pairs={{0,16},{16,32},{32,48},{48,64},{64,80},{80,96},{96,112},{112,128},... | collective-permute-start | bytes 786440 | tf_op jit(solution)/shard_map/while/body/eval_jaxpr/ppermute | solution.py:17
  297.0 9.8 %collective-permute-start = (f32[4,128,128]{2,1,0:T(8,128)S(1)}, f32[4,128,128]{2,1,0:T(8,128)S(1)}, u32[]{:S(2)}, u32[]{:S(2)}) collective-permute-start(f32[4,128,128]{2,1,0:T(8,128)S(1)} %multiply_add_fusion.3), channel_id=1, source_target_pairs={{0,16},{16,32},{32,48},{48,64},{64,80},{80,96},{96,112},{112,128},... | collective-permute-start | bytes 786440 | tf_op jit(solution)/shard_map/while/body/eval_jaxpr/ppermute | solution.py:17
  306.9 9.8 %collective-permute-start = (f32[4,128,128]{2,1,0:T(8,128)S(1)}, f32[4,128,128]{2,1,0:T(8,128)S(1)}, u32[]{:S(2)}, u32[]{:S(2)}) collective-permute-start(f32[4,128,128]{2,1,0:T(8,128)S(1)} %multiply_add_fusion.3), channel_id=1, source_target_pairs={{0,16},{16,32},{32,48},{48,64},{64,80},{80,96},{96,112},{112,128},... | collective-permute-start | bytes 786440 | tf_op jit(solution)/shard_map/while/body/eval_jaxpr/ppermute | solution.py:17
  316.8 9.8 %collective-permute-start = (f32[4,128,128]{2,1,0:T(8,128)S(1)}, f32[4,128,128]{2,1,0:T(8,128)S(1)}, u32[]{:S(2)}, u32[]{:S(2)}) collective-permute-start(f32[4,128,128]{2,1,0:T(8,128)S(1)} %multiply_add_fusion.3), channel_id=1, source_target_pairs={{0,16},{16,32},{32,48},{48,64},{64,80},{80,96},{96,112},{112,128},... | collective-permute-start | bytes 786440 | tf_op jit(solution)/shard_map/while/body/eval_jaxpr/ppermute | solution.py:17
  327.4 37.3 %copy-start.3 = (f32[512]{0:T(512)S(1)}, f32[512]{0:T(512)}, u32[]{:S(2)}) copy-start(f32[512]{0:T(512)} %param.18) | copy-start | bytes 6148
Sparse Core Ops, SparseCore 0:
  11.7 64.7 all-gather.4
  79.7 60.1 all-gather.6
